TPU v7x, 256 devices: a whole 4x4x8 slice. The times are simulated.
256 devices in a mesh: group: 4 (over y), shard: 16 (over x_hi, z), tensor: 4 (over x_lo, core).
Axes of the slice: x: 4 (x_hi: 2, x_lo: 2; x = x_hi * 2 + x_lo), y: 4, z: 8, core: 2. Of those that a mesh axis runs over, the one named last changes fastest.
Arguments:
- group_weights: bfloat16 [4, 8, 1024, 8704], P('group', None, None, ('shard', 'tensor')), may hold values from -6 to 6
- anchor: float32 [8, 1024, 16, 4, 136], P(None, ('group', 'shard'), None, 'tensor'), may hold values from -6 to 6
- momentum: float32 [8, 1024, 16, 4, 136], P(None, ('group', 'shard'), None, 'tensor'), may hold values from -6 to 6
- group_embedding: bfloat16 [4, 32000, 1024], P('group', 'shard', 'tensor'), may hold values from -6 to 6
- emb_anchor: float32 [32000, 1024], P('shard', 'tensor'), may hold values from -6 to 6
- emb_momentum: float32 [32000, 1024], P('shard', 'tensor'), may hold values from -6 to 6
- basis: float32 [1024, 64], P('tensor'), may hold values from -0.1875 to 0.1875
Outputs:
- new_weights: bfloat16 [8, 1024, 8704], P(None, None, ('shard', 'tensor'))
- new_anchor: float32 [8, 1024, 16, 4, 136], P(None, ('group', 'shard'), None, 'tensor')
- new_momentum: float32 [8, 1024, 16, 4, 136], P(None, ('group', 'shard'), None, 'tensor')
- new_embedding: bfloat16 [32000, 1024], P('shard', 'tensor')
- new_emb_anchor: float32 [32000, 1024], P('shard', 'tensor')
- new_emb_momentum: float32 [32000, 1024], P('shard', 'tensor')
All inputs are finite; a program needn't handle non-finite values.
Results may differ from a plain program's by a relative error of at most 0.012.
Values may be sent and summed in bfloat16 or wider, within the bound.
No kernel may reach another device: no remote copies, remote signals or barrier semaphores. Data moves between devices by JAX's collectives and lax.ppermute only.
A program may use at most 128 MiB of HBM per device.

v0:
```python
import jax
import jax.numpy as jnp
from jax import lax
from jax.sharding import PartitionSpec as P

outer_rate = 0.7
momentum_decay = 0.9


def per_device(group_weights, anchor, momentum, group_embedding, emb_anchor, emb_momentum, basis):
    groups = lax.axis_size("group")
    layers = group_weights.shape[1]
    width = group_weights.shape[2]
    block = group_weights.shape[3]
    local_weights = group_weights[0]
    part = lax.psum_scatter(
        local_weights.astype(jnp.float32).astype(jnp.bfloat16),
        "group",
        scatter_dimension=1,
        tiled=True,
    ).astype(jnp.float32)
    part = part.reshape(layers, part.shape[1], 1, 1, block)
    summed = lax.all_to_all(part, "shard", split_axis=1, concat_axis=2, tiled=True)
    delta = anchor - summed / groups
    moved = momentum_decay * momentum + delta
    stepped = anchor - outer_rate * (delta + momentum_decay * moved)
    stepped_half = stepped.astype(jnp.bfloat16)
    columns = lax.all_to_all(stepped_half, "shard", split_axis=2, concat_axis=1, tiled=True)
    whole = lax.all_gather(columns, "group", axis=1, tiled=True)
    new_weights = whole.reshape(layers, width, block)
    local_embedding = group_embedding[0].astype(jnp.float32)
    emb_sum = lax.psum(local_embedding.astype(jnp.bfloat16), "group").astype(jnp.float32)
    difference = emb_anchor - emb_sum / groups
    coef = lax.psum(jnp.dot(difference, basis, precision=lax.Precision.HIGHEST), "tensor")
    emb_delta = jnp.dot(coef, basis.T, precision=lax.Precision.HIGHEST)
    emb_moved = momentum_decay * emb_momentum + emb_delta
    emb_stepped = emb_anchor - outer_rate * (emb_delta + momentum_decay * emb_moved)
    return (new_weights, stepped, moved, emb_stepped.astype(jnp.bfloat16), emb_stepped, emb_moved)


def solution(mesh):
    return jax.shard_map(
        per_device,
        mesh=mesh,
        in_specs=(
            P("group", None, None, ("shard", "tensor")),
            P(None, ("group", "shard"), None, "tensor", None),
            P(None, ("group", "shard"), None, "tensor", None),
            P("group", "shard", "tensor"),
            P("shard", "tensor"),
            P("shard", "tensor"),
            P("tensor", None),
        ),
        out_specs=(
            P(None, None, ("shard", "tensor")),
            P(None, ("group", "shard"), None, "tensor", None),
            P(None, ("group", "shard"), None, "tensor", None),
            P("shard", "tensor"),
            P("shard", "tensor"),
            P("shard", "tensor"),
        ),
        check_vma=False,
    )
```

profile of v0, /device:TPU:1, one launch (start us, length us, event | category | flops | bytes accessed | tf_op | source)
XLA Modules:
  0.0 260.1 jit_solution(16609563485341192564)
XLA Ops:
  7.2 6.8 %copy.20 = bf16[1,8,1024,136]{3,1,2,0:T(8,128)(2,1)} copy(bf16[1,8,1024,136]{2,3,1,0:T(8,128)(2,1)} %param.7) | data formatting | bytes 4456448 | tf_op args[0]
  14.0 53.3 %reduce-scatter.2.cloned.1.call-done = bf16[8,256,136]{2,0,1:T(8,128)(2,1)} async-done(((bf16[8,1024,136]{2,0,1:T(8,128)(2,1)}), bf16[8,256,136]{2,0,1:T(8,128)(2,1)}) %reduce-scatter.2.cloned.1.call-update) | async-done | bytes 557072 | tf_op jit(solution)/shard_map/reduce_scatter | solution.py:16
  67.3 2.7 %bitcast_convert_fusion = f32[8,256,1,1,136]{4,0,3,2,1:T(8,128)} fusion(bf16[8,256,136]{2,0,1:T(8,128)(2,1)} %reduce-scatter.2.cloned.1.call-done), kind=kLoop, calls=%fused_computation.11 | loop fusion | flops 278528 | bytes 1671168 | tf_op jit(solution)/shard_map/reshape | solution.py:22
  70.0 9.2 %all-to-all-start = ((f32[8,256,1,1,136]{4,0,3,2,1:T(8,128)}), f32[8,256,1,1,136]{4,0,3,2,1:T(8,128)S(1)}, u32[]{:S(2)}, u32[]{:S(2)}) async-start(f32[8,256,1,1,136]{4,0,3,2,1:T(8,128)} %bitcast_convert_fusion), calls=%async_computation.1 | async-start | bytes 4194304 | tf_op jit(solution)/shard_map/all_to_all | solution.py:23
  79.3 0.0 all-reduce.3.cloned.1.call-start
  79.3 0.7 all-reduce.3.cloned.1.call-update
  80.0 48.4 %all-to-all-done = f32[8,256,1,1,136]{4,0,3,2,1:T(8,128)S(1)} async-done(((f32[8,256,1,1,136]{4,0,3,2,1:T(8,128)}), f32[8,256,1,1,136]{4,0,3,2,1:T(8,128)S(1)}, u32[]{:S(2)}, u32[]{:S(2)}) %all-to-all-start) | async-done | bytes 1114144 | tf_op jit(solution)/shard_map/all_to_all | solution.py:23
  128.5 0.7 copy_multiply_fusion.1
  129.2 0.9 copy-done.2
  130.1 0.6 copy-done.3
  130.7 5.1 %fusion.8 = (bf16[8,16,16,1,136]{4,1,2,0,3:T(8,128)(2,1)S(1)}, f32[8,16,16,1,136]{4,1,2,0,3:T(8,128)}, f32[8,16,16,1,136]{4,1,2,0,3:T(8,128)S(1)}) fusion(f32[8,16,16,1,136]{4,3,2,1,0:T(1,128)S(1)} %copy-done.2, f32[8,16,16,1,136]{4,1,2,0,3:T(8,128)S(1)} %bitcast.19, f32[8,16,16,1,136]{4,3,2,1,0:T(1,128)S(1)} %copy-done.3), kind=kLoop, calls=%fused_computation.15 | loop fusion | flops 2228224 | bytes 6127616 | tf_op jit(solution)/shard_map/convert_element_type | solution.py:27
  135.8 1.1 copy.25
  136.9 7.1 %all-to-all-start.1 = ((bf16[8,16,16,1,136]{4,1,0,3,2:T(8,128)(2,1)}), bf16[8,16,16,1,136]{4,1,0,3,2:T(8,128)(2,1)S(1)}, u32[]{:S(2)}, u32[]{:S(2)}) async-start(bf16[8,16,16,1,136]{4,1,0,3,2:T(8,128)(2,1)} %copy.25), calls=%async_computation.2 | async-start | bytes 2097152 | tf_op jit(solution)/shard_map/all_to_all | solution.py:28
  144.0 0.0 all-reduce.5.cloned.1.call-start
  144.1 4.8 %fusion.1 = f32[2000,64]{0,1:T(8,128)} fusion(f32[256,64]{0,1:T(8,128)S(1)} %copy-done, f32[2000,256]{1,0:T(8,128)} %param.11, bf16[2000,256]{1,0:T(8,128)(2,1)} %all-reduce.3.cloned.1.call-done), kind=kOutput, calls=%fused_computation.6 | convolution fusion | flops 394752000 | bytes 3649536 | tf_op jit(solution)/shard_map/dot_general | solution.py:34
  148.9 0.2 all-gather.2.cloned.1.call-start
  149.1 21.9 %all-to-all-done.1 = bf16[8,16,16,1,136]{4,1,0,3,2:T(8,128)(2,1)S(1)} async-done(((bf16[8,16,16,1,136]{4,1,0,3,2:T(8,128)(2,1)}), bf16[8,16,16,1,136]{4,1,0,3,2:T(8,128)(2,1)S(1)}, u32[]{:S(2)}, u32[]{:S(2)}) %all-to-all-start.1) | async-done | bytes 557088 | tf_op jit(solution)/shard_map/all_to_all | solution.py:28
  171.1 1.1 copy.26
  172.2 22.1 %all-reduce.5.cloned.1.call-done = f32[2000,64]{0,1:T(8,128)} async-done(((f32[2000,64]{0,1:T(8,128)}), f32[2000,64]{0,1:T(8,128)}) %all-reduce.5.cloned.1.call-update) | async-done | bytes 512016 | tf_op jit(solution)/shard_map/psum | solution.py:34
  194.3 6.9 %fusion.7 = (bf16[2000,256]{1,0:T(8,128)(2,1)}, f32[2000,256]{1,0:T(8,128)}, f32[2000,256]{1,0:T(8,128)}) fusion(f32[2000,256]{1,0:T(8,128)} %param.11, f32[2000,256]{1,0:T(8,128)} %param.12, f32[2000,64]{0,1:T(8,128)} %all-reduce.5.cloned.1.call-done, f32[256,64]{0,1:T(8,128)S(1)} %copy-done), kind=kOutput, calls=%fused_computation.14 | convolution fusion | flops 396800000 | bytes 9793536 | tf_op jit(solution)/shard_map/dot_general | solution.py:35
  201.3 3.7 %copy.28 = f32[8,16,16,1,136]{4,3,2,1,0:T(1,128)} copy(f32[8,16,16,1,136]{4,1,2,0,3:T(8,128)S(1)} %copy-done.1) | data formatting | bytes 2228224
  205.0 3.7 %copy.29 = f32[8,16,16,1,136]{4,3,2,1,0:T(1,128)} copy(f32[8,16,16,1,136]{4,1,2,0,3:T(8,128)S(1)} %get-tuple-element.23) | data formatting | bytes 2228224
  208.7 39.0 %all-gather.2.cloned.1.call-done = bf16[8,1024,1,1,136]{4,1,0,3,2:T(8,128)(2,1)} async-done(((bf16[8,256,1,1,136]{4,1,0,3,2:T(8,128)(2,1)}), bf16[8,1024,1,1,136]{4,1,0,3,2:T(8,128)(2,1)}) %all-gather.2.cloned.1.call-update) | async-done | bytes 2228240 | tf_op jit(solution)/shard_map/all_gather | solution.py:29
  247.7 5.9 %copy.27 = bf16[8,1024,136]{1,2,0:T(8,128)(2,1)} copy(bf16[8,1024,136]{2,1,0:T(8,128)(2,1)} %bitcast.20) | data formatting | bytes 4456448
  (11 shorter events, 0.1 us)
Async XLA Ops:
  7.2 136.9 %copy-start = (f32[256,64]{0,1:T(8,128)S(1)}, f32[256,64]{0,1:T(8,128)}, u32[]{:S(2)}) copy-start(f32[256,64]{0,1:T(8,128)} %param.13) | copy-start | bytes 196612
  7.2 60.1 %reduce-scatter.2.cloned.1.call-start = ((), (), s32[]{:S(2)}) async-start(), calls=%async_computation.3 | async-start | bytes 5242880 | tf_op jit(solution)/shard_map/reduce_scatter | solution.py:16
  70.0 58.4 %all-to-all-start = ((f32[8,256,1,1,136]{4,0,3,2,1:T(8,128)}), f32[8,256,1,1,136]{4,0,3,2,1:T(8,128)S(1)}, u32[]{:S(2)}, u32[]{:S(2)}) async-start(f32[8,256,1,1,136]{4,0,3,2,1:T(8,128)} %bitcast_convert_fusion), calls=%async_computation.1 | async-start | bytes 4194304 | tf_op jit(solution)/shard_map/all_to_all | solution.py:23
  79.3 64.8 %all-reduce.3.cloned.1.call-start = ((), (), s32[]{:S(2)}) async-start(), calls=%async_computation.5 | async-start | bytes 2048000 | tf_op jit(solution)/shard_map/psum | solution.py:32
  128.5 1.6 copy-start.2
  128.5 2.3 copy-start.3
  136.9 34.2 %all-to-all-start.1 = ((bf16[8,16,16,1,136]{4,1,0,3,2:T(8,128)(2,1)}), bf16[8,16,16,1,136]{4,1,0,3,2:T(8,128)(2,1)S(1)}, u32[]{:S(2)}, u32[]{:S(2)}) async-start(bf16[8,16,16,1,136]{4,1,0,3,2:T(8,128)(2,1)} %copy.25), calls=%async_computation.2 | async-start | bytes 2097152 | tf_op jit(solution)/shard_map/all_to_all | solution.py:28
  144.0 50.3 %all-reduce.5.cloned.1.call-start = ((), (), s32[]{:S(2)}) async-start(), calls=%async_computation.6 | async-start | bytes 1048576 | tf_op jit(solution)/shard_map/psum | solution.py:34
  148.9 98.8 %all-gather.2.cloned.1.call-start = ((), (), s32[]{:S(2)}) async-start(), calls=%async_computation.4 | async-start | bytes 5242880 | tf_op jit(solution)/shard_map/all_gather | solution.py:29
  194.3 6.9 %copy-start.1 = (f32[8,16,16,1,136]{4,1,2,0,3:T(8,128)S(1)}, f32[8,16,16,1,136]{4,1,2,0,3:T(8,128)}, u32[]{:S(2)}) copy-start(f32[8,16,16,1,136]{4,1,2,0,3:T(8,128)} %get-tuple-element.22) | copy-start | bytes 3342340
Sparse Core Ops, SparseCore 0:
  14.1 53.1 reduce-scatter.1
  82.4 50.1 all-reduce.2
  149.0 45.2 all-reduce.4
  196.6 51.0 all-gather.1
where the time goes:
time: 261 us; the launch traced here: 260 us
  waiting for transfers between devices  186 us (71%)
  local copies, waits for them, and re-layouts  23.8 us (9%)
  starting transfers between devices  16.7 us (6%)
  between operations  13.8 us (5%)
  matrix products  11.7 us (4%)
  other arithmetic  8.55 us (3%)
    reduce_scatter x1, waiting for transfers between devices, per_device(): lax.psum_scatter(local_weights.astype(jnp.float32).astype(jnp.bfloat16),...  53.3 us
    all_to_all x1, waiting for transfers between devices, per_device(): lax.all_to_all(part, 'shard', split_axis=1, concat_axis=2, tiled=True)  48.4 us
    all_gather x1, waiting for transfers between devices, per_device(): whole = lax.all_gather(columns, 'group', axis=1, tiled=True)  39 us
    psum x1, waiting for transfers between devices, per_device(): lax.psum(jnp.dot(difference, basis, precision=lax.Precision.HIGHEST), 'te...  22.1 us
    all_to_all x1, waiting for transfers between devices, per_device(): lax.all_to_all(stepped_half, 'shard', split_axis=2, concat_axis=1, tiled=...  21.9 us
    unnamed x12, local copies, waits for them, and re-layouts  21.6 us
    all_to_all x1, starting transfers between devices, per_device(): lax.all_to_all(part, 'shard', split_axis=1, concat_axis=2, tiled=True)  9.24 us
    all_to_all x1, starting transfers between devices, per_device(): lax.all_to_all(stepped_half, 'shard', split_axis=2, concat_axis=1, tiled=...  7.1 us
  transfers between devices with their start and end apart: 6, of which 5 were waited for; matrix products, arithmetic and copies ran while one was open for 10% of the time, Pallas kernels for 0%

commit v1 on v0

--- a/solution.py
+++ b/solution.py
@@ -18,9 +18,9 @@
         "group",
         scatter_dimension=1,
         tiled=True,
-    ).astype(jnp.float32)
+    )
     part = part.reshape(layers, part.shape[1], 1, 1, block)
-    summed = lax.all_to_all(part, "shard", split_axis=1, concat_axis=2, tiled=True)
+    summed = lax.all_to_all(part, "shard", split_axis=1, concat_axis=2, tiled=True).astype(jnp.float32)
     delta = anchor - summed / groups
     moved = momentum_decay * momentum + delta
     stepped = anchor - outer_rate * (delta + momentum_decay * moved)
@@ -28,10 +28,9 @@
     columns = lax.all_to_all(stepped_half, "shard", split_axis=2, concat_axis=1, tiled=True)
     whole = lax.all_gather(columns, "group", axis=1, tiled=True)
     new_weights = whole.reshape(layers, width, block)
-    local_embedding = group_embedding[0].astype(jnp.float32)
-    emb_sum = lax.psum(local_embedding.astype(jnp.bfloat16), "group").astype(jnp.float32)
-    difference = emb_anchor - emb_sum / groups
-    coef = lax.psum(jnp.dot(difference, basis, precision=lax.Precision.HIGHEST), "tensor")
+    local_difference = emb_anchor - group_embedding[0].astype(jnp.float32)
+    partial = jnp.dot(local_difference, basis, precision=lax.Precision.HIGHEST)
+    coef = lax.psum(partial, ("group", "tensor")) * (1.0 / groups)
     emb_delta = jnp.dot(coef, basis.T, precision=lax.Precision.HIGHEST)
     emb_moved = momentum_decay * emb_momentum + emb_delta
     emb_stepped = emb_anchor - outer_rate * (emb_delta + momentum_decay * emb_moved)

time: 261 us -> 276 us (1.057)
  blocking collectives: 0 us -> 35.6 us
  starting transfers between devices: 16.7 us -> 6.68 us
  waiting for transfers between devices: 186 us -> 177 us
  other arithmetic: 8.55 us -> 5.36 us
    psum x2 -> x1, waiting for transfers between devices: 22.2 us -> 102 us  [per_device(): coef = lax.psum(partial, ('group', 'tensor')) * (1.0 / groups)]
    all_to_all x1 -> x0, waiting for transfers between devices: 48.4 us -> none  [per_device(): lax.all_to_all(part, 'shard', split_axis=1, concat_axis=2, tiled=True)]
    all_gather x1, waiting for transfers between devices: 39 us -> 0.01 us  [per_device(): whole = lax.all_gather(columns, 'group', axis=1, tiled=True)]
    all_to_all x0 -> x1, blocking collectives: none -> 35.6 us  [per_device(): lax.all_to_all(part, 'shard', split_axis=1, concat_axis=2, tiled=True)]
    all_to_all x1 -> x0, starting transfers between devices: 9.24 us -> none  [per_device(): lax.all_to_all(part, 'shard', split_axis=1, concat_axis=2, tiled=True)]
  transfers between devices with their start and end apart: 6 -> 4, of which waited for: 5 -> 3; matrix products, arithmetic and copies ran while one was open for 10% -> 7% of each run, Pallas kernels for 0% -> 0%
where the time goes in v1:
time: 276 us
  waiting for transfers between devices  177 us (64%)
  blocking collectives  35.6 us (13%)
  local copies, waits for them, and re-layouts  23.6 us (9%)
  between operations  15.5 us (6%)
  matrix products  11.7 us (4%)
  starting transfers between devices  6.68 us (2%)
  other arithmetic  5.36 us (2%)
    psum x1, waiting for transfers between devices, per_device(): coef = lax.psum(partial, ('group', 'tensor')) * (1.0 / groups)  102 us
    reduce_scatter x1, waiting for transfers between devices, per_device(): lax.psum_scatter(local_weights.astype(jnp.float32).astype(jnp.bfloat16),...  53.3 us
    all_to_all x1, blocking collectives, per_device(): lax.all_to_all(part, 'shard', split_axis=1, concat_axis=2, tiled=True)  35.6 us
    all_to_all x1, waiting for transfers between devices, per_device(): lax.all_to_all(stepped_half, 'shard', split_axis=2, concat_axis=1, tiled=...  21.4 us
    unnamed x12, local copies, waits for them, and re-layouts  21.4 us
    dot_general x1, matrix products, per_device(): emb_delta = jnp.dot(coef, basis.T, precision=lax.Precision.HIGHEST)  6.95 us
    all_to_all x1, starting transfers between devices, per_device(): lax.all_to_all(stepped_half, 'shard', split_axis=2, concat_axis=1, tiled=...  6.37 us
  transfers between devices with their start and end apart: 4, of which 3 were waited for; matrix products, arithmetic and copies ran while one was open for 7% of the time, Pallas kernels for 0%

profile of v1, /device:TPU:1, one launch (start us, length us, event | category | flops | bytes accessed | tf_op | source)
XLA Modules:
  0.0 275.6 jit_solution(16387879592642991854)
XLA Ops:
  8.0 0.0 copy-start
  8.0 0.0 reduce-scatter.2.cloned.1.call-start
  8.1 6.8 %copy.20 = bf16[1,8,1024,136]{3,1,2,0:T(8,128)(2,1)} copy(bf16[1,8,1024,136]{2,3,1,0:T(8,128)(2,1)} %param.7) | data formatting | bytes 4456448 | tf_op args[0]
  14.8 0.0 reduce-scatter.2.cloned.1.call-update
  14.8 53.3 %reduce-scatter.2.cloned.1.call-done = bf16[8,256,136]{2,0,1:T(8,128)(2,1)} async-done(((bf16[8,1024,136]{2,0,1:T(8,128)(2,1)}), bf16[8,256,136]{2,0,1:T(8,128)(2,1)}) %reduce-scatter.2.cloned.1.call-update) | async-done | bytes 557072 | tf_op jit(solution)/shard_map/reduce_scatter | solution.py:16
  68.1 35.6 %all_to_all.27 = bf16[8,256,1,1,136]{4,0,3,2,1:T(8,128)(2,1)S(1)} all-to-all(bf16[8,256,1,1,136]{4,0,3,2,1:T(8,128)(2,1)} %bitcast.25), channel_id=1, replica_groups=mesh['group'=4,'shard'=16,'tensor'=4] {'shard'}, dimensions={1} | all-to-all | bytes 1114112 | tf_op jit(solution)/shard_map/all_to_all | solution.py:23
  103.8 0.3 convert_multiply_fusion
  104.0 1.3 copy-done.2
  105.3 5.1 %fusion.8 = (bf16[8,16,16,1,136]{4,1,2,0,3:T(8,128)(2,1)S(1)}, f32[8,16,16,1,136]{4,1,2,0,3:T(8,128)}, f32[8,16,16,1,136]{4,1,2,0,3:T(8,128)S(1)}) fusion(f32[8,16,16,1,136]{4,3,2,1,0:T(1,128)S(1)} %copy-done.2, f32[8,16,16,1,136]{4,1,2,0,3:T(8,128)S(1)} %bitcast.21, f32[8,16,16,1,136]{4,3,2,1,0:T(1,128)S(1)} %copy-done.3), kind=kLoop, calls=%fused_computation.15 | loop fusion | flops 2228224 | bytes 6127616 | tf_op jit(solution)/shard_map/convert_element_type | solution.py:27
  110.4 1.1 copy.25
  111.5 6.4 %all-to-all-start.1 = ((bf16[8,16,16,1,136]{4,1,0,3,2:T(8,128)(2,1)}), bf16[8,16,16,1,136]{4,1,0,3,2:T(8,128)(2,1)S(1)}, u32[]{:S(2)}, u32[]{:S(2)}) async-start(bf16[8,16,16,1,136]{4,1,0,3,2:T(8,128)(2,1)} %copy.25), calls=%async_computation.2 | async-start | bytes 2097152 | tf_op jit(solution)/shard_map/all_to_all | solution.py:28
  117.9 0.0 all-reduce.2.cloned.1.call-start
  118.0 4.7 %fusion.1 = f32[2000,64]{0,1:T(8,128)} fusion(f32[256,64]{0,1:T(8,128)S(1)} %copy-done, f32[2000,256]{1,0:T(8,128)} %param.11, bf16[1,2000,256]{2,1,0:T(8,128)(2,1)} %param.10), kind=kOutput, calls=%fused_computation.5 | convolution fusion | flops 394240000 | bytes 3649536 | tf_op jit(solution)/shard_map/dot_general | solution.py:32
  122.7 0.0 all-reduce.2.cloned.1.call-update
  122.7 0.2 all-gather.2.cloned.1.call-start
  123.0 21.4 %all-to-all-done.1 = bf16[8,16,16,1,136]{4,1,0,3,2:T(8,128)(2,1)S(1)} async-done(((bf16[8,16,16,1,136]{4,1,0,3,2:T(8,128)(2,1)}), bf16[8,16,16,1,136]{4,1,0,3,2:T(8,128)(2,1)S(1)}, u32[]{:S(2)}, u32[]{:S(2)}) %all-to-all-start.1) | async-done | bytes 557088 | tf_op jit(solution)/shard_map/all_to_all | solution.py:28
  144.4 1.1 copy.26
  145.5 0.0 all-gather.2.cloned.1.call-update
  145.5 102.4 %all-reduce.2.cloned.1.call-done = f32[2000,64]{0,1:T(8,128)} async-done(((f32[2000,64]{0,1:T(8,128)}), f32[2000,64]{0,1:T(8,128)}) %all-reduce.2.cloned.1.call-update) | async-done | bytes 512016 | tf_op jit(solution)/shard_map/psum | solution.py:33
  247.9 7.0 %fusion.7 = (bf16[2000,256]{1,0:T(8,128)(2,1)}, f32[2000,256]{1,0:T(8,128)}, f32[2000,256]{1,0:T(8,128)}) fusion(f32[2000,256]{1,0:T(8,128)} %param.11, f32[2000,256]{1,0:T(8,128)} %param.12, f32[256,64]{0,1:T(8,128)S(1)} %copy-done, f32[2000,64]{0,1:T(8,128)} %all-reduce.2.cloned.1.call-done), kind=kOutput, calls=%fused_computation.14 | convolution fusion | flops 396928000 | bytes 9793536 | tf_op jit(solution)/shard_map/dot_general | solution.py:34
  254.8 0.0 copy-done.1
  254.8 3.7 %copy.28 = f32[8,16,16,1,136]{4,3,2,1,0:T(1,128)} copy(f32[8,16,16,1,136]{4,1,2,0,3:T(8,128)S(1)} %copy-done.1) | data formatting | bytes 2228224
  258.5 3.7 %copy.29 = f32[8,16,16,1,136]{4,3,2,1,0:T(1,128)} copy(f32[8,16,16,1,136]{4,1,2,0,3:T(8,128)S(1)} %get-tuple-element.23) | data formatting | bytes 2228224
  262.3 5.9 %copy.27 = bf16[8,1024,136]{1,2,0:T(8,128)(2,1)} copy(bf16[8,1024,136]{2,1,0:T(8,128)(2,1)} %bitcast.22) | data formatting | bytes 4456448
  (6 shorter events, 0.0 us)
Async XLA Ops:
  8.0 110.0 %copy-start = (f32[256,64]{0,1:T(8,128)S(1)}, f32[256,64]{0,1:T(8,128)}, u32[]{:S(2)}) copy-start(f32[256,64]{0,1:T(8,128)} %param.13) | copy-start | bytes 196612
  8.0 60.1 %reduce-scatter.2.cloned.1.call-start = ((), (), s32[]{:S(2)}) async-start(), calls=%async_computation.3 | async-start | bytes 5242880 | tf_op jit(solution)/shard_map/reduce_scatter | solution.py:16
  68.1 35.9 %copy-start.3 = (f32[8,16,16,1,136]{4,3,2,1,0:T(1,128)S(1)}, f32[8,16,16,1,136]{4,3,2,1,0:T(1,128)}, u32[]{:S(2)}) copy-start(f32[8,16,16,1,136]{4,3,2,1,0:T(1,128)} %param.8) | copy-start | bytes 3342340
  103.8 1.6 copy-start.2
  111.5 32.9 %all-to-all-start.1 = ((bf16[8,16,16,1,136]{4,1,0,3,2:T(8,128)(2,1)}), bf16[8,16,16,1,136]{4,1,0,3,2:T(8,128)(2,1)S(1)}, u32[]{:S(2)}, u32[]{:S(2)}) async-start(bf16[8,16,16,1,136]{4,1,0,3,2:T(8,128)(2,1)} %copy.25), calls=%async_computation.2 | async-start | bytes 2097152 | tf_op jit(solution)/shard_map/all_to_all | solution.py:28
  117.9 129.9 %all-reduce.2.cloned.1.call-start = ((), (), s32[]{:S(2)}) async-start(), calls=%async_computation.5 | async-start | bytes 1048576 | tf_op jit(solution)/shard_map/psum | solution.py:33
  122.7 139.5 %all-gather.2.cloned.1.call-start = ((), (), s32[]{:S(2)}) async-start(), calls=%async_computation.4 | async-start | bytes 5242880 | tf_op jit(solution)/shard_map/all_gather | solution.py:29
  247.9 7.0 %copy-start.1 = (f32[8,16,16,1,136]{4,1,2,0,3:T(8,128)S(1)}, f32[8,16,16,1,136]{4,1,2,0,3:T(8,128)}, u32[]{:S(2)}) copy-start(f32[8,16,16,1,136]{4,1,2,0,3:T(8,128)} %get-tuple-element.22) | copy-start | bytes 3342340
Sparse Core Ops, SparseCore 0:
  15.0 53.1 reduce-scatter.1
  145.6 49.0 all-gather.1
Sparse Core Ops, SparseCore 1:
  122.8 125.0 all-reduce.1
